TPU v7x, 256 devices: a whole 4x4x8 slice. The times are simulated.
256 devices in a mesh: req: 64 (over z, x, core), kv: 4 (over y).
Axes of the slice: x: 4, y: 4, z: 8, core: 2. Of those that a mesh axis runs over, the one named last changes fastest.
Arguments:
- residual_in: bfloat16 [128, 2560], P('req', 'kv'), may hold values from -8 to 8
- queries: bfloat16 [128, 2560], P('req', 'kv'), may hold values from -480 to 480
- fresh_token_keys: bfloat16 [128, 512], P('req', 'kv'), may hold values from -6 to 6
- fresh_token_values: bfloat16 [128, 512], P('req', 'kv'), may hold values from -6 to 6
- cached_key_slots: bfloat16 [128, 4096, 512], P('req', None, 'kv'), may hold values from -6 to 6
- cached_value_slots: bfloat16 [128, 4096, 512], P('req', None, 'kv'), may hold values from -6 to 6
- lengths: int32 [128], replicated, may hold values from 1 to 4096, as said below
- slot_order: int32 [128], replicated, may hold values from 0 to 127, as said below
- out_proj: bfloat16 [2560, 2560], P('kv'), may hold values from -0.5 to 0.5
- norm_gain: bfloat16 [2560], P('kv'), may hold values from 0.5 to 1.5
- expert_ids: int32 [128, 6], replicated, may hold values from 0 to 63, all different within a row; in each aligned block of 128 rows (0 to 127, 128 to 255, ...) at most 24 rows name the same one
- gate_values: float32 [128, 6], replicated, may hold values from 0.1 to 0.5
- gate_proj: bfloat16 [64, 2560, 1536], P('req', None, 'kv'), may hold values from -0.125 to 0.125
- up_proj: bfloat16 [64, 2560, 1536], P('req', None, 'kv'), may hold values from -0.125 to 0.125
- down_proj: bfloat16 [64, 1536, 2560], P('req', 'kv'), may hold values from -0.15625 to 0.15625
Outputs:
- layer_out: bfloat16 [128, 2560], P('req', 'kv')
Inputs may be any that keep to these rules, and one draw needn't show every extreme that they name: `lengths`: each request's count of cached positions; some request has exactly 4096. A permutation of the requests: slot s serves request slot_order[s], and cached_key_slots[s], cached_value_slots[s] hold that request's cache. Requests sorted by decreasing length are dealt to the 64 groups of 2 consecutive slots, one round forward, the next backward. `expert_ids`: each token names 6 different experts; no expert is named by more than 24 tokens, a bound that some block reaches.
All inputs are finite; a program needn't handle non-finite values.
Results may differ from a plain program's by a relative error of at most 0.012.
Values may be sent and summed in bfloat16 or wider, within the bound.
No kernel may reach another device: no remote copies, remote signals or barrier semaphores. Data moves between devices by JAX's collectives and lax.ppermute only.
A program may use at most 64 MiB of HBM per device.

v0:
```python
import math
import jax
import jax.numpy as jnp
from jax import lax
from jax.sharding import PartitionSpec as P

COMBINE = "a2a"


def per_device(
    residual_in,
    queries,
    fresh_token_keys,
    fresh_token_values,
    cached_key_slots,
    cached_value_slots,
    lengths,
    slot_order,
    out_proj,
    norm_gain,
    expert_ids,
    gate_values,
    gate_proj,
    up_proj,
    down_proj,
):
    req_count = lax.axis_size("req")
    kv_count = lax.axis_size("kv")
    req_index = lax.axis_index("req")
    kv_index = lax.axis_index("kv")
    per_dev = residual_in.shape[0]
    head_dim = fresh_token_keys.shape[1]
    col_count = residual_in.shape[1]
    total_reqs = lengths.shape[0]
    model_width = out_proj.shape[1]
    q_width = queries.shape[1]
    packed = jnp.concatenate([queries, fresh_token_keys, fresh_token_values, residual_in], axis=1)
    all_packed = lax.all_gather(packed, "req", axis=0, tiled=True)
    served = lax.dynamic_slice_in_dim(slot_order, req_index * per_dev, per_dev)
    mine = all_packed[served]
    query_rows = mine[:, :q_width].reshape(per_dev, -1, head_dim)
    self_key_row = mine[:, q_width : q_width + head_dim]
    self_value_row = mine[:, q_width + head_dim : q_width + 2 * head_dim]
    residual_rows = mine[:, q_width + 2 * head_dim :]
    live_len = lengths[served]
    inv_root = 1.0 / math.sqrt(head_dim)
    scores = (
        jnp.einsum("rqd,rld->rql", query_rows, cached_key_slots, preferred_element_type=jnp.float32)
        * inv_root
    )
    positions = jnp.arange(cached_key_slots.shape[1])
    scores = jnp.where((positions[None, :] < live_len[:, None])[:, None, :], scores, -1e30)
    own_score = (
        jnp.einsum("rqd,rd->rq", query_rows, self_key_row, preferred_element_type=jnp.float32)
        * inv_root
    )
    highest = jnp.maximum(jnp.max(scores, axis=2), own_score)
    weights = jnp.exp(scores - highest[:, :, None])
    own_weight = jnp.exp(own_score - highest)
    totals = jnp.sum(weights, axis=2) + own_weight
    numerator = jnp.einsum(
        "rql,rld->rqd",
        weights.astype(jnp.bfloat16),
        cached_value_slots,
        preferred_element_type=jnp.float32,
    )
    own_low = lax.optimization_barrier(own_weight.astype(jnp.bfloat16)).astype(jnp.float32)
    numerator = numerator + own_low[:, :, None] * self_value_row.astype(jnp.float32)[:, None, :]
    attended = (numerator / totals[:, :, None]).astype(jnp.bfloat16).reshape(per_dev, -1)
    projected = jnp.dot(attended, out_proj, preferred_element_type=jnp.float32)
    col_start = kv_index * col_count
    own_cols = jnp.concatenate(
        [residual_rows.astype(jnp.float32), norm_gain.astype(jnp.float32)[None, :]], axis=0
    )
    summed_in = jnp.concatenate(
        [projected, jnp.zeros((1, model_width), jnp.float32)], axis=0
    ) + lax.dynamic_update_slice(
        jnp.zeros((per_dev + 1, model_width), jnp.float32), own_cols, (0, col_start)
    )
    summed = lax.psum(summed_in, "kv")
    hidden = summed[:per_dev]
    gain = summed[per_dev]
    squares = jnp.sum(hidden * hidden, axis=1)
    normed = (hidden * lax.rsqrt(squares / model_width + 1e-06)[:, None] * gain).astype(
        jnp.bfloat16
    )
    by_slot = lax.all_gather(normed, "req", axis=0, tiled=True)
    slot_of = (
        jnp.zeros((total_reqs,), jnp.int32)
        .at[slot_order]
        .set(jnp.arange(total_reqs, dtype=jnp.int32))
    )
    local_count = gate_proj.shape[0]
    capacity = min(2 * total_reqs * expert_ids.shape[1] // (local_count * req_count), total_reqs)
    expert = req_index * local_count + 0
    named_here = expert_ids == expert
    token_gate = jnp.sum(jnp.where(named_here, gate_values, 0.0), axis=1)
    uses_expert = jnp.any(named_here, axis=1)
    picked = jnp.nonzero(uses_expert, size=capacity, fill_value=0)[0].astype(jnp.int32)
    valid_rows = jnp.arange(capacity) < jnp.sum(uses_expert.astype(jnp.int32))
    row_block = by_slot[slot_of[picked]]
    gate_h = jnp.dot(row_block, gate_proj[0], preferred_element_type=jnp.float32)
    up_h = jnp.dot(row_block, up_proj[0], preferred_element_type=jnp.float32)
    inner_act = (jax.nn.silu(gate_h) * up_h).astype(jnp.bfloat16)
    outputs = jnp.dot(inner_act, down_proj[0], preferred_element_type=jnp.float32)
    row_gate = jnp.where(valid_rows, token_gate[picked], 0.0)
    weighted = outputs * row_gate[:, None]
    weighted = lax.psum_scatter(weighted, "kv", scatter_dimension=1, tiled=True)
    own_hidden = lax.dynamic_slice_in_dim(hidden, col_start, col_count, axis=1)
    combined = (
        jnp.zeros((total_reqs, col_count), jnp.float32)
        .at[picked]
        .add(weighted)
        .at[served]
        .add(own_hidden)
    )
    if COMBINE == "rs":
        layer_rows = lax.psum_scatter(combined, "req", scatter_dimension=0, tiled=True)
    else:
        layer_rows = jnp.sum(
            lax.all_to_all(
                combined.reshape(req_count, per_dev, col_count), "req", 0, 0, tiled=False
            ),
            axis=0,
        )
    return layer_rows.astype(jnp.bfloat16)


def solution(mesh):
    in_specs = (
        P("req", "kv"),
        P("req", "kv"),
        P("req", "kv"),
        P("req", "kv"),
        P("req", None, "kv"),
        P("req", None, "kv"),
        P(),
        P(),
        P("kv", None),
        P("kv"),
        P(),
        P(),
        P("req", None, "kv"),
        P("req", None, "kv"),
        P("req", "kv", None),
    )
    out_specs = P("req", "kv")
    return jax.shard_map(
        per_device, mesh=mesh, in_specs=in_specs, out_specs=out_specs, check_vma=False
    )
```

profile of v0, /device:TPU:1, one launch (start us, length us, event | category | flops | bytes accessed | tf_op | source)
XLA Modules:
  0.0 225.2 jit_solution(8981033612592452208)
XLA Ops:
  6.5 0.9 compare_select_fusion.4
  8.0 0.7 maximum_bitcast_fusion
  8.7 57.9 %all-gather = bf16[64,2,1536]{2,1,0:T(2,128)(2,1)} all-gather(bf16[1,2,1536]{2,1,0:T(2,128)(2,1)S(1)} %maximum_bitcast_fusion), channel_id=1, replica_groups=mesh['req'=64,'kv'=4] {'req'}, dimensions={0}, use_global_device_ids=true | all-gather | bytes 399360 | tf_op jit(solution)/shard_map/all_gather | solution.py:38
  66.6 1.9 reshape.232
  68.5 1.6 gather_fusion.1
  70.2 1.3 gather_fusion
  71.7 2.3 %fusion.51 = (f32[2,5]{1,0:T(2,128)S(1)}, f32[2,5,4096]{2,1,0:T(8,128)S(1)}) fusion(bf16[2,5,128]{2,1,0:T(8,128)(2,1)S(1)} %reshape.151, bf16[2,4096,128]{2,1,0:T(8,128)(2,1)} %param.19, pred[2,4096]{1,0:T(4,128)(4,1)S(1)} %iota_compare_fusion), kind=kOutput, calls=%fused_computation.85 | convolution fusion | flops 10608630 | bytes 2271784 | tf_op jit(solution)/shard_map/rqd,rld->rql/dot_general | solution.py:48
  76.1 2.0 fusion.16
  78.8 13.9 %psum.7 = f32[3,2560]{1,0:T(4,128)S(1)} all-reduce(f32[3,2560]{1,0:T(4,128)S(1)} %add_dynamic-update-slice_fusion), channel_id=1, replica_groups=mesh['req'=64,'kv'=4] {'kv'}, use_global_device_ids=true, to_apply=%region_7.8 | all-reduce | flops 7680 | bytes 61440 | tf_op jit(solution)/shard_map/psum | solution.py:80
  93.6 56.6 %all-gather.1 = bf16[64,2,2560]{2,1,0:T(2,128)(2,1)} all-gather(bf16[1,2,2560]{2,1,0:T(2,128)(2,1)S(1)} %fusion.34), channel_id=1, replica_groups=mesh['req'=64,'kv'=4] {'req'}, dimensions={0}, use_global_device_ids=true | all-gather | bytes 665600 | tf_op jit(solution)/shard_map/all_gather | solution.py:87
  150.2 2.7 %reshape.234 = bf16[128,2560]{1,0:T(8,128)(2,1)} reshape(bf16[64,2,2560]{2,1,0:T(2,128)(2,1)} %all-gather.1) | data formatting | bytes 1310720
  153.3 1.4 scatter_custom_fusion
  154.9 0.8 fusion.32
  155.6 1.0 scatter_custom_fusion.1
  157.5 0.7 gather_fusion.4
  158.9 1.9 gather_fusion.3
  160.8 1.9 fusion.4
  162.8 3.8 %convolution_multiply_fusion.1 = f32[24,2560]{1,0:T(8,128)} fusion(bf16[1,384,2560]{2,1,0:T(8,128)(2,1)} %param.29, bf16[24,2560]{1,0:T(8,128)(2,1)S(1)} %gather_fusion.3, bf16[1,2560,384]{2,1,0:T(8,128)(2,1)} %param.28, f32[24]{0:T(128)S(1)} %compare_select_fusion.5, f32[24,384]{1,0:T(8,128)S(1)} %fusion.4), kind=kOutput, calls=%fused_computation.11 | convolution fusion | flops 94488576 | bytes 4337760 | tf_op jit(solution)/shard_map/dot_general | solution.py:105
  166.5 16.9 %reduce-scatter.2.cloned.1.call-done = f32[24,640]{1,0:T(8,128)} async-done(((f32[24,2560]{1,0:T(8,128)}), f32[24,640]{1,0:T(8,128)}) %reduce-scatter.2.cloned.1.call-update) | async-done | bytes 61456 | tf_op jit(solution)/shard_map/reduce_scatter | solution.py:108
  183.5 1.7 scatter_custom_fusion.2
  185.2 2.4 %scatter_custom_fusion.3 = f32[128,640]{1,0:T(8,128)} fusion(f32[128,640]{1,0:T(8,128)} %scatter_custom_fusion.2, s32[2]{0:T(128)} %copy-done.3, f32[2,2560]{1,0:T(2,128)S(1)} %get-tuple-element.7, s32[]{:T(128)} %constant.31.clone.1, s32[]{:T(128)S(6)} %select_n.104), kind=kCustom, calls=%fused_computation.54 | custom fusion | flops 1280 | bytes 333316 | tf_op jit(solution)/shard_map/scatter-add | solution.py:115
  187.6 1.9 reshape.153
  189.5 27.2 %all_to_all.5 = f32[64,2,640]{2,1,0:T(2,128)} all-to-all(f32[64,2,640]{2,1,0:T(2,128)} %reshape.153), channel_id=1, replica_groups=mesh['req'=64,'kv'=4] {'req'}, dimensions={0} | all-to-all | bytes 655360 | tf_op jit(solution)/shard_map/all_to_all | solution.py:121
  216.7 1.7 reduce_sum.53
  (47 shorter events, 6.5 us)
Async XLA Ops:
  6.5 71.6 %copy-start = (bf16[640,2560]{1,0:T(8,128)(2,1)S(1)}, bf16[640,2560]{1,0:T(8,128)(2,1)}, u32[]{:S(2)}) copy-start(bf16[640,2560]{1,0:T(8,128)(2,1)} %param.23) | copy-start | bytes 9830404
  6.5 176.9 %reduce-scatter.2.cloned.1.call-start = ((), (), s32[]{:S(2)}) async-start(), calls=%async_computation.2 | async-start | bytes 307200 | tf_op jit(solution)/shard_map/reduce_scatter | solution.py:108
  7.4 0.5 copy-start.3
  78.1 14.7 %copy-start.1 = (f32[128,6]{0,1:T(8,128)S(1)}, f32[128,6]{0,1:T(8,128)}, u32[]{:S(2)}) copy-start(f32[128,6]{0,1:T(8,128)} %param.26) | copy-start | bytes 9220
  78.1 14.7 %copy-start.2 = (s32[128,6]{0,1:T(8,128)S(1)}, s32[128,6]{0,1:T(8,128)}, u32[]{:S(2)}) copy-start(s32[128,6]{0,1:T(8,128)} %param.25) | copy-start | bytes 9220
  78.2 14.7 %copy-start.4 = (s32[128]{0:T(128)S(1)}, s32[128]{0:T(128)}, u32[]{:S(2)}) copy-start(s32[128]{0:T(128)} %param.22) | copy-start | bytes 1540
Sparse Core Ops, SparseCore 0:
  166.7 16.7 reduce-scatter.1
where the time goes:
time: 226 us; the launch traced here: 225 us
  blocking collectives  156 us (69%)
  waiting for transfers between devices  17 us (8%)
  local copies, waits for them, and re-layouts  15.3 us (7%)
  between operations  13.6 us (6%)
  other arithmetic  13.1 us (6%)
  matrix products  10.7 us (5%)
    all_gather x1, blocking collectives, per_device(): all_packed = lax.all_gather(packed, 'req', axis=0, tiled=True)  57.9 us
    all_gather x1, blocking collectives, per_device(): by_slot = lax.all_gather(normed, 'req', axis=0, tiled=True)  56.6 us
    all_to_all x1, blocking collectives, per_device(): lax.all_to_all(combined.reshape(req_count, per_dev, col_count), 'req', 0,...  27.2 us
    reduce_scatter x1, waiting for transfers between devices, per_device(): weighted = lax.psum_scatter(weighted, 'kv', scatter_dimension=1, tiled=True)  16.9 us
    psum x1, blocking collectives, per_device(): summed = lax.psum(summed_in, 'kv')  13.9 us
    unnamed x12, local copies, waits for them, and re-layouts  5.18 us
  transfers between devices with their start and end apart: 1, of which 1 were waited for; matrix products, arithmetic and copies ran while one was open for 0% of the time, Pallas kernels for 0%

commit v1 on v0

--- a/solution.py
+++ b/solution.py
@@ -1,10 +1,20 @@
+import functools
 import math
 import jax
 import jax.numpy as jnp
 from jax import lax
 from jax.sharding import PartitionSpec as P
+from jax.lax import all_gather
 
 COMBINE = "a2a"
+
+
+def follow_domain(original, mesh_dim):
+    a_next = all_gather(original, mesh_dim)
+    return jnp.sum(a_next, 0)
+
+
+cards_try_all = functools.partial(follow_domain, mesh_dim="kv")
 
 
 def per_device(
@@ -77,7 +87,7 @@
     ) + lax.dynamic_update_slice(
         jnp.zeros((per_dev + 1, model_width), jnp.float32), own_cols, (0, col_start)
     )
-    summed = lax.psum(summed_in, "kv")
+    summed = cards_try_all(summed_in)
     hidden = summed[:per_dev]
     gain = summed[per_dev]
     squares = jnp.sum(hidden * hidden, axis=1)

time: 226 us -> 218 us (0.965)
  blocking collectives: 156 us -> 151 us
    psum x1 -> x0, blocking collectives: 13.9 us -> none  [per_device(): summed = lax.psum(summed_in, 'kv')]
    all_gather x0 -> x1, blocking collectives: none -> 10.2 us  [follow_domain(): a_next = all_gather(original, mesh_dim)]
    unnamed x12 -> x14, local copies, waits for them, and re-layouts: 5.18 us -> 4.73 us
where the time goes in v1:
time: 218 us
  blocking collectives  151 us (69%)
  waiting for transfers between devices  18.3 us (8%)
  local copies, waits for them, and re-layouts  14.2 us (7%)
  between operations  13.6 us (6%)
  other arithmetic  12 us (6%)
  matrix products  9.19 us (4%)
    all_gather x1, blocking collectives, per_device(): all_packed = lax.all_gather(packed, 'req', axis=0, tiled=True)  57.9 us
    all_gather x1, blocking collectives, per_device(): by_slot = lax.all_gather(normed, 'req', axis=0, tiled=True)  55.2 us
    all_to_all x1, blocking collectives, per_device(): lax.all_to_all(combined.reshape(req_count, per_dev, col_count), 'req', 0,...  27.2 us
    reduce_scatter x1, waiting for transfers between devices, per_device(): weighted = lax.psum_scatter(weighted, 'kv', scatter_dimension=1, tiled=True)  18.2 us
    all_gather x1, blocking collectives, follow_domain(): a_next = all_gather(original, mesh_dim)  10.2 us
    unnamed x14, local copies, waits for them, and re-layouts  4.73 us
  transfers between devices with their start and end apart: 1, of which 1 were waited for; matrix products, arithmetic and copies ran while one was open for 0% of the time, Pallas kernels for 0%

profile of v1, /device:TPU:1, one launch (start us, length us, event | category | flops | bytes accessed | tf_op | source)
XLA Modules:
  0.0 217.7 jit_solution(16429583218855168579)
XLA Ops:
  6.5 0.9 compare_select_fusion.4
  7.4 0.8 maximum_bitcast_fusion
  8.3 57.9 %all-gather = bf16[64,2,1536]{2,1,0:T(2,128)(2,1)} all-gather(bf16[1,2,1536]{2,1,0:T(2,128)(2,1)S(1)} %maximum_bitcast_fusion), channel_id=1, replica_groups=mesh['req'=64,'kv'=4] {'req'}, dimensions={0}, use_global_device_ids=true | all-gather | bytes 399360 | tf_op jit(solution)/shard_map/all_gather | solution.py:48
  66.2 1.9 reshape.234
  68.1 1.6 gather_fusion.1
  69.7 1.3 gather_fusion
  71.2 2.4 %fusion.54 = (f32[2,5]{1,0:T(2,128)S(1)}, f32[2,5,4096]{2,1,0:T(8,128)S(1)}) fusion(bf16[2,5,128]{2,1,0:T(8,128)(2,1)S(1)} %reshape.153, bf16[2,4096,128]{2,1,0:T(8,128)(2,1)} %param.19, pred[2,4096]{1,0:T(4,128)(4,1)S(1)} %iota_compare_fusion), kind=kOutput, calls=%fused_computation.89 | convolution fusion | flops 10608630 | bytes 2271784 | tf_op jit(solution)/shard_map/rqd,rld->rql/dot_general | solution.py:58
  75.1 10.2 %all_gather.17 = f32[4,3,2560]{2,1,0:T(4,128)S(1)} all-gather(f32[1,3,2560]{2,1,0:T(4,128)S(1)} %fusion.36), channel_id=1, replica_groups=mesh['req'=64,'kv'=4] {'kv'}, dimensions={0}, use_global_device_ids=true | all-gather | bytes 153600 | tf_op jit(solution)/shard_map/all_gather | solution.py:13
  86.3 55.2 %all-gather.1 = bf16[64,2,2560]{2,1,0:T(2,128)(2,1)} all-gather(bf16[1,2,2560]{2,1,0:T(2,128)(2,1)S(1)} %fusion.37), channel_id=1, replica_groups=mesh['req'=64,'kv'=4] {'req'}, dimensions={0}, use_global_device_ids=true | all-gather | bytes 665600 | tf_op jit(solution)/shard_map/all_gather | solution.py:97
  141.5 2.7 %reshape.236 = bf16[128,2560]{1,0:T(8,128)(2,1)} reshape(bf16[64,2,2560]{2,1,0:T(2,128)(2,1)} %all-gather.1) | data formatting | bytes 1310720
  144.6 1.4 scatter_custom_fusion
  146.2 0.8 fusion.32
  147.0 1.0 scatter_custom_fusion.1
  147.9 0.7 gather_fusion.2
  148.9 0.7 gather_fusion.4
  150.2 1.9 gather_fusion.3
  152.2 1.9 fusion.4
  154.1 3.8 %convolution_multiply_fusion.1 = f32[24,2560]{1,0:T(8,128)} fusion(bf16[1,384,2560]{2,1,0:T(8,128)(2,1)} %param.29, bf16[24,2560]{1,0:T(8,128)(2,1)S(1)} %gather_fusion.3, bf16[1,2560,384]{2,1,0:T(8,128)(2,1)} %param.28, f32[24]{0:T(128)S(1)} %compare_select_fusion.5, f32[24,384]{1,0:T(8,128)S(1)} %fusion.4), kind=kOutput, calls=%fused_computation.11 | convolution fusion | flops 94488576 | bytes 4337760 | tf_op jit(solution)/shard_map/dot_general | solution.py:115
  157.9 18.2 %reduce-scatter.2.cloned.1.call-done = f32[24,640]{1,0:T(8,128)} async-done(((f32[24,2560]{1,0:T(8,128)}), f32[24,640]{1,0:T(8,128)}) %reduce-scatter.2.cloned.1.call-update) | async-done | bytes 61456 | tf_op jit(solution)/shard_map/reduce_scatter | solution.py:118
  176.1 1.7 scatter_custom_fusion.2
  177.8 2.2 %scatter_custom_fusion.3 = f32[128,640]{1,0:T(8,128)} fusion(f32[128,640]{1,0:T(8,128)} %scatter_custom_fusion.2, s32[2]{0:T(128)S(1)} %compare_select_fusion.4, f32[2,2560]{1,0:T(2,128)S(1)} %get-tuple-element.7, s32[]{:T(128)} %constant.33.clone.1, s32[]{:T(128)S(6)} %select_n.104), kind=kCustom, calls=%fused_computation.58 | custom fusion | flops 1280 | bytes 333316 | tf_op jit(solution)/shard_map/scatter-add | solution.py:125
  180.1 1.9 reshape.155
  182.0 27.2 %all_to_all.5 = f32[64,2,640]{2,1,0:T(2,128)} all-to-all(f32[64,2,640]{2,1,0:T(2,128)} %reshape.155), channel_id=1, replica_groups=mesh['req'=64,'kv'=4] {'req'}, dimensions={0} | all-to-all | bytes 655360 | tf_op jit(solution)/shard_map/all_to_all | solution.py:131
  209.2 1.7 reduce_sum.63
  (50 shorter events, 4.0 us)
Async XLA Ops:
  6.5 67.8 %copy-start = (bf16[640,2560]{1,0:T(8,128)(2,1)S(1)}, bf16[640,2560]{1,0:T(8,128)(2,1)}, u32[]{:S(2)}) copy-start(bf16[640,2560]{1,0:T(8,128)(2,1)} %param.23) | copy-start | bytes 9830404
  6.5 169.6 %reduce-scatter.2.cloned.1.call-start = ((), (), s32[]{:S(2)}) async-start(), calls=%async_computation.2 | async-start | bytes 307200 | tf_op jit(solution)/shard_map/reduce_scatter | solution.py:118
  71.0 2.9 %copy-start.1 = (bf16[2,4096,128]{2,1,0:T(8,128)(2,1)S(1)}, bf16[2,4096,128]{2,1,0:T(8,128)(2,1)}, u32[]{:S(2)}) copy-start(bf16[2,4096,128]{2,1,0:T(8,128)(2,1)} %param.20) | copy-start | bytes 6291460
  74.4 0.7 copy-start.4
  74.4 11.1 %copy-start.2 = (f32[128,6]{0,1:T(8,128)S(1)}, f32[128,6]{0,1:T(8,128)}, u32[]{:S(2)}) copy-start(f32[128,6]{0,1:T(8,128)} %param.26) | copy-start | bytes 9220
  74.4 11.1 %copy-start.3 = (s32[128,6]{0,1:T(8,128)S(1)}, s32[128,6]{0,1:T(8,128)}, u32[]{:S(2)}) copy-start(s32[128,6]{0,1:T(8,128)} %param.25) | copy-start | bytes 9220
  74.4 11.1 %copy-start.5 = (s32[128]{0:T(128)S(1)}, s32[128]{0:T(128)}, u32[]{:S(2)}) copy-start(s32[128]{0:T(128)} %param.22) | copy-start | bytes 1540
Sparse Core Ops, SparseCore 0:
  158.0 18.0 reduce-scatter.1
